TPU v7x, 32 devices: a whole 2x2x4 slice. The times are simulated.
32 devices in a mesh: gx: 8 (over y, x, core), gy: 4 (over z).
Axes of the slice: x: 2, y: 2, z: 4, core: 2. Of those that a mesh axis runs over, the one named last changes fastest.
Arguments:
- temp_start: float32 [8, 1024, 2048], P(None, ('gx', 'gy')), may hold values from -6 to 6
- heat_input: float32 [8, 1024, 2048], P(None, ('gx', 'gy')), may hold values from -3 to 3
- lateral: float32 [8], replicated, may hold values from 0.03 to 0.15
- vertical: float32 [7], replicated, may hold values from 0.03 to 0.15
- weighting: float32 [8], replicated, may hold values from -1 to 1
- modulus: float32 [1024, 2048], P('gx', 'gy'), may hold values from 0.3 to 3
- warp_prev: float32 [1024, 2048], P('gx', 'gy'), may hold values from -6 to 6
- joint_cell: int32 [65536], P(('gx', 'gy')), may hold values from 0 to 65535
- joint_owner: int32 [65536, 1], P(('gx', 'gy')), may hold values from 0 to 31; in each aligned block of 2048 rows (0 to 2047, 2048 to 4095, ...) at most 192 rows name the same one
- joint_strain: float32 [2, 32, 6144], P(None, ('gx', 'gy')), may hold values from -4 to 4
- joint_resist: float32 [32, 6144], P(('gx', 'gy')), may hold values from 1 to 2
Outputs:
- warpage: float32 [1024, 2048], P('gx', 'gy')
- strain_next: float32 [2, 32, 6144], P(None, ('gx', 'gy'))
- resist_next: float32 [32, 6144], P(('gx', 'gy'))
Inputs may be any that keep to these rules, and one draw needn't show every extreme that they name: `joint_owner`: among the 2048 joints of one device at most 192 have the same owner, and on some device exactly 192 do.
All inputs are finite; a program needn't handle non-finite values.
Results may differ from a plain program's by a relative error of at most 0.0003.
Values sent between devices are 32-bit elements; how exact they have to be, the bound alone decides.
No kernel may reach another device: no remote copies, remote signals or barrier semaphores. Data moves between devices by JAX's collectives and lax.ppermute only.
A program may use at most 320 MiB of HBM per device.

v0:
```python
import jax
import jax.numpy as jnp
from jax import lax
from jax.sharding import PartitionSpec as P

STEPS = 2
SWEEPS = 3
stiffness = 0.2
shear_mod = 0.6
rate_scale = 0.5
sat_level = 2.5
sat_power = 0.3
harden = 2.0
FLAT = ("gx", "gy")


def exchange(last, leading, axis):
    count = lax.axis_size(axis)
    up = [(i, i + 1) for i in range(count - 1)]
    down = [(j, i) for i, j in up]
    return (lax.ppermute(last, axis, up), lax.ppermute(leading, axis, down))


def with_halo(array, sides, width):
    for axis, dim in sides:
        length = array.shape[dim]
        last = lax.slice_in_dim(array, length - width, length, axis=dim)
        leading = lax.slice_in_dim(array, 0, width, axis=dim)
        before, after = exchange(last, leading, axis)
        array = jnp.concatenate([before, array, after], axis=dim)
    return array


def thermal_step(ext, heat_rows, lateral, vertical):
    cols = jnp.pad(ext, ((0, 0), (0, 0), (1, 1)))
    center = ext[:, 1:-1]
    lap = ext[:, 2:] + ext[:, :-2] + cols[:, 1:-1, 2:] + cols[:, 1:-1, :-2] - 4.0 * center
    flux = vertical[:, None, None] * (center[1:] - center[:-1])
    vert = jnp.pad(flux, ((0, 1), (0, 0), (0, 0))) - jnp.pad(flux, ((1, 0), (0, 0), (0, 0)))
    return center + lateral[:, None, None] * lap + vert + heat_rows


def moment_of(field, weighting):
    total = weighting[0] * field[0]
    for layer in range(1, field.shape[0]):
        total = total + weighting[layer] * field[layer]
    return total


def sweep(w_pad, e_pad, load):
    center = e_pad[1:-1, 1:-1]
    e_up = 0.5 * (center + e_pad[:-2, 1:-1])
    e_down = 0.5 * (center + e_pad[2:, 1:-1])
    e_left = 0.5 * (center + e_pad[1:-1, :-2])
    e_right = 0.5 * (center + e_pad[1:-1, 2:])
    numer = (
        load
        + e_up * w_pad[:-2, 1:-1]
        + e_down * w_pad[2:, 1:-1]
        + e_left * w_pad[1:-1, :-2]
        + e_right * w_pad[1:-1, 2:]
    )
    denom = stiffness + e_up + e_down + e_left + e_right
    return numer / denom


def anand(strain, resist, recv):
    total, inelastic = (strain[0], strain[1])
    increment, theta, live = (recv[0], recv[1], recv[2])
    total_new = total + increment
    arrhen = jnp.exp(2.0 - 2.0 / (1.0 + 0.1 * theta * theta))
    hyper = jnp.sinh(shear_mod * (total_new - inelastic) / resist)
    rate = rate_scale * arrhen * hyper * jnp.abs(hyper)
    inelastic_new = inelastic + rate
    target = sat_level * jnp.power(1.0 + jnp.abs(rate) / arrhen, sat_power)
    resist_new = resist + harden * (1.0 - resist / target) * jnp.abs(rate)
    keep = live > 0.5
    strain_out = jnp.stack(
        [jnp.where(keep, total_new, total), jnp.where(keep, inelastic_new, inelastic)]
    )
    return (strain_out, jnp.where(keep, resist_new, resist))


def thermal(temp, heat, lateral, vertical):
    devices = lax.axis_size(FLAT)
    t = lax.axis_index(FLAT)
    rows = temp.shape[1]
    h = STEPS
    last = jnp.concatenate([temp[:, rows - h :], heat[:, rows - (h - 1) :]], axis=1)
    leading = jnp.concatenate([temp[:, :h], heat[:, : h - 1]], axis=1)
    before, after = exchange(last, leading, FLAT)
    ext = jnp.concatenate([before[:, :h], temp, after[:, :h]], axis=1)
    heat_ext = jnp.concatenate([before[:, h:], heat, after[:, h:]], axis=1)
    for step in range(1, STEPS + 1):
        r = STEPS - step
        heat_rows = heat_ext[:, h - 1 - r : h - 1 - r + rows + 2 * r]
        ext = thermal_step(ext, heat_rows, lateral, vertical)
        if r > 0:
            g = t * rows + jnp.arange(-r, rows + r)
            inside = (g >= 0) & (g < devices * rows)
            ext = jnp.where(inside[None, :, None], ext, 0.0)
    return ext


def relay(load, top, width):
    n_gy = lax.axis_size("gy")
    rows, cols = load.shape
    cm = cols // n_gy
    before, after = exchange(load[rows - width :], load[:width], FLAT)
    load_ext = jnp.concatenate([before, load, after], axis=0)
    lp = jnp.pad(load_ext, ((0, 0), (width, width)))
    tp = jnp.pad(top, ((width, width), (width, width)))
    both = jnp.stack([lp, tp])
    send = jnp.stack([both[:, :, k * cm : k * cm + cm + 2 * width] for k in range(n_gy)])
    recv = lax.all_to_all(send, "gy", split_axis=0, concat_axis=0, tiled=True)
    parts = []
    for k in range(n_gy):
        lo = 0 if k == 0 else width
        hi = rows + 2 * width if k == n_gy - 1 else rows + width
        parts.append(recv[k, 0, lo:hi])
    load_m = jnp.concatenate(parts, axis=0)
    top_m = jnp.concatenate(
        [recv[k, 1, width : rows + width, width : cm + width] for k in range(n_gy)], axis=0
    )
    return (load_m, top_m)


def joint_ranks(owners, devices):
    count = owners.shape[0]
    block = 128 if count % 128 == 0 else count
    nb = count // block
    onehot = (owners[:, None] == jnp.arange(devices, dtype=jnp.int32)[None, :]).astype(jnp.float32)
    oh = onehot.reshape(nb, block, devices)
    ar = jnp.arange(block)
    tri = (ar[:, None] >= ar[None, :]).astype(jnp.float32)
    within = jnp.einsum("ij,bjd->bid", tri, oh, precision=lax.Precision.HIGHEST)
    totals = within[:, -1, :]
    ab = jnp.arange(nb)
    stri = (ab[:, None] > ab[None, :]).astype(jnp.float32)
    offs = jnp.dot(stri, totals, precision=lax.Precision.HIGHEST)
    cum = (within + offs[:, None, :]).reshape(count, devices)
    return jnp.sum(cum * onehot, axis=1).astype(jnp.int32) - 1


def body(
    temp_start,
    heat_input,
    lateral,
    vertical,
    weighting,
    modulus,
    warp_prev,
    joint_cell,
    joint_owner,
    joint_strain,
    joint_resist,
):
    devices = lax.axis_size(FLAT)
    n_gx, n_gy = (lax.axis_size("gx"), lax.axis_size("gy"))
    gi, gj = (lax.axis_index("gx"), lax.axis_index("gy"))
    rm, cm = warp_prev.shape
    wm = with_halo(jnp.stack([warp_prev, modulus]), (("gx", 1), ("gy", 2)), SWEEPS)
    owners = joint_owner[:, 0]
    capacity = joint_resist.shape[1] // devices
    slots = owners * capacity + joint_ranks(owners, devices)
    temp = thermal(temp_start, heat_input, lateral, vertical)
    load_t = moment_of(temp, weighting)
    load, top = relay(load_t, temp[-1], SWEEPS - 1)
    warp = wm[0]
    mod_ext = wm[1]
    for step in range(1, SWEEPS + 1):
        r = SWEEPS - step
        off = SWEEPS - (r + 1)
        e_pad = mod_ext[off : off + rm + 2 * r + 2, off : off + cm + 2 * r + 2]
        lo = SWEEPS - 1 - r
        ld = load[lo : lo + rm + 2 * r, lo : lo + cm + 2 * r]
        warp = sweep(warp, e_pad, ld)
        if r > 0:
            gr = gi * rm + jnp.arange(-r, rm + r)
            gc = gj * cm + jnp.arange(-r, cm + r)
            inside = ((gr >= 0) & (gr < n_gx * rm))[:, None] & ((gc >= 0) & (gc < n_gy * cm))[
                None, :
            ]
            warp = jnp.where(inside, warp, 0.0)
    fields = jnp.stack([(warp - warp_prev).reshape(-1), top.reshape(-1)])
    picked = fields[:, joint_cell]
    values = jnp.concatenate([picked, jnp.ones_like(picked[:1])], axis=0)
    outgoing = jnp.zeros((3, devices * capacity), jnp.float32).at[:, slots].set(values)
    incoming = lax.all_to_all(outgoing, FLAT, split_axis=1, concat_axis=1, tiled=True)
    strain_next, resist_next = anand(joint_strain, joint_resist, incoming[:, None, :])
    return (warp, strain_next, resist_next)


def solution(mesh):
    return jax.shard_map(
        body,
        mesh=mesh,
        in_specs=(
            P(None, FLAT, None),
            P(None, FLAT, None),
            P(),
            P(),
            P(),
            P("gx", "gy"),
            P("gx", "gy"),
            P(FLAT),
            P(FLAT, None),
            P(None, FLAT, None),
            P(FLAT, None),
        ),
        out_specs=(P("gx", "gy"), P(None, FLAT, None), P(FLAT, None)),
        check_vma=False,
    )
```

profile of v0, /device:TPU:0, one launch (start us, length us, event | category | flops | bytes accessed | tf_op | source)
XLA Modules:
  0.0 136.8 jit_solution(4110263155972718763)
XLA Ops:
  0.7 1.4 %fusion.88 = (f32[8,2,2048]{2,1,0:T(2,128)S(1)}, f32[8,2,2048]{2,1,0:T(2,128)S(1)}) fusion(f32[8,32,2048]{2,1,0:T(8,128)} %param.11), kind=kLoop, calls=%fused_computation.191 | loop fusion | bytes 524288 | tf_op jit(solution)/shard_map/slice | solution.py:89
  2.1 1.3 fusion.89
  3.5 5.0 %collective-permute-start = (f32[8,3,2048]{2,1,0:T(4,128)S(1)}, f32[8,3,2048]{2,1,0:T(4,128)S(1)}, u32[]{:S(2)}, u32[]{:S(2)}) collective-permute-start(f32[8,3,2048]{2,1,0:T(4,128)S(1)} %pad_maximum_fusion.5), channel_id=1, source_target_pairs={{0,1},{1,2},{2,3},{3,4},{4,5},{5,6},{6,7},{7,8},{8,9},{9,10},{10,1... | collective-permute-start | bytes 589832 | tf_op jit(solution)/shard_map/ppermute | solution.py:21
  8.6 1.3 collective-permute-start.1
  9.9 0.8 pad_maximum_fusion.14
  10.7 4.7 %collective-permute-start.4 = (f32[2,3,512]{2,1,0:T(4,128)S(1)}, f32[2,3,512]{2,1,0:T(4,128)S(1)}, u32[]{:S(2)}, u32[]{:S(2)}) collective-permute-start(f32[2,3,512]{2,1,0:T(4,128)S(1)} %get-tuple-element.31), channel_id=1, source_target_pairs={{0,4},{4,8},{8,12},{12,16},{16,20},{20,24},{24,28},{1,5},{5,9},{9,... | collective-permute-start | bytes 36872 | tf_op jit(solution)/shard_map/ppermute | solution.py:21
  15.4 1.3 collective-permute-start.5
  16.7 1.6 %fusion.94 = (f32[1]{0:T(128)}, f32[1]{0:T(128)}, f32[1]{0:T(128)}, f32[1]{0:T(128)}, f32[1]{0:T(128)}, /*index=5*/f32[1]{0:T(128)}, f32[1]{0:T(128)}, f32[1]{0:T(128)}) fusion(f32[8]{0:T(128)} %param.15), kind=kLoop, calls=%fused_computation.197 | loop fusion | bytes 64 | tf_op jit(solution)/shard_map/slice | solution.py:44
  18.3 0.9 convolution_bitcast_fusion
  19.2 0.3 slice_reduce_fusion
  19.6 0.2 select_reduce_fusion
  19.9 3.4 %collective-permute-done.1 = f32[8,3,2048]{2,1,0:T(4,128)S(1)} collective-permute-done((f32[8,3,2048]{2,1,0:T(4,128)S(1)}, f32[8,3,2048]{2,1,0:T(4,128)S(1)}, u32[]{:S(2)}, u32[]{:S(2)}) %collective-permute-start.1) | collective-permute-done | bytes 196640 | tf_op jit(solution)/shard_map/ppermute | solution.py:21
  23.4 0.4 pad_maximum_fusion
  23.8 0.4 fusion.8
  24.3 1.0 copy-done.1
  25.3 3.0 %fusion.7 = f32[8,34,2048]{2,1,0:T(8,128)S(1)} fusion(f32[8,36,2048]{2,1,0:T(8,128)S(1)} %pad_maximum_fusion, f32[8,2,2048]{2,1,0:T(2,128)S(1)} %slice.403, f32[8,32,2048]{2,1,0:T(8,128)S(1)} %copy-done, f32[8,2,2048]{2,1,0:T(2,128)S(1)} %slice.402, f32[8,1,2048]{2,1,0:T(1,128)S(1)} %slice.408, f32[8,32,2048]{2,1,0:T(8,128)S(1)} %copy-done.1, ...), kind=kLoop, calls=%fused_computation.13 | loop fusion | flops 8355840 | bytes 14353408 | tf_op jit(solution)/shard_map/jit(_where)/select_n | solution.py:101
  28.4 0.4 fusion.16
  28.8 1.9 %fusion.15 = f32[8,32,2048]{2,1,0:T(8,128)S(1)} fusion(f32[8,32,2048]{2,1,0:T(8,128)S(1)} %copy-done.1, f32[8,34,2048]{2,1,0:T(8,128)S(1)} %fusion.7, f32[7,32,2048]{2,1,0:T(8,128)S(1)} %fusion.16, f32[8]{0:T(128)S(1)} %copy-done.9), kind=kLoop, calls=%fused_computation.24 | loop fusion | flops 5242880 | bytes 14942720 | tf_op jit(solution)/shard_map/add | solution.py:40
  30.7 5.2 %fusion.54 = f32[32,2048]{1,0:T(8,128)S(1)} fusion(f32[8,32,2048]{2,1,0:T(8,128)S(1)} %fusion.15, f32[]{:T(128)} %bitcast.8, f32[]{:T(128)} %bitcast.6, f32[]{:T(128)} %bitcast.5, f32[]{:T(128)} %bitcast.4, f32[]{:T(128)} %bitcast.3, f32[]{:T(128)} %bitcast.2, f32[]{:T(128)} %bitcast.1, f32[]{:T(128)} %bitcast), kind=kLoop, calls=%fused_computation.109 | loop fusion | flops 983040 | bytes 2359328 | tf_op jit(solution)/shard_map/add | solution.py:46
  35.9 2.5 %collective-permute-start.2 = (f32[2,2048]{1,0:T(2,128)S(1)}, f32[2,2048]{1,0:T(2,128)S(1)}, u32[]{:S(2)}, u32[]{:S(2)}) collective-permute-start(f32[2,2048]{1,0:T(2,128)S(1)} %get-tuple-element.33), channel_id=1, source_target_pairs={{0,1},{1,2},{2,3},{3,4},{4,5},{5,6},{6,7},{7,8},{8,9},{9,10},{10,1... | collective-permute-start | bytes 49160 | tf_op jit(solution)/shard_map/ppermute | solution.py:21
  38.4 1.3 collective-permute-start.3
  39.9 0.2 stack.44
  40.1 3.9 %collective-permute-done.3 = f32[2,2048]{1,0:T(2,128)S(1)} collective-permute-done((f32[2,2048]{1,0:T(2,128)S(1)}, f32[2,2048]{1,0:T(2,128)S(1)}, u32[]{:S(2)}, u32[]{:S(2)}) %collective-permute-start.3) | collective-permute-done | bytes 16416 | tf_op jit(solution)/shard_map/ppermute | solution.py:21
  44.0 0.2 fusion.41
  44.3 0.3 copy.17
  44.6 0.7 fusion.65
  45.3 1.2 pad_maximum_fusion.1
  46.5 5.4 %all-to-all-start = ((f32[4,2,36,516]{3,1,2,0:T(2,128)}), f32[4,2,36,516]{3,1,2,0:T(2,128)S(1)}, u32[]{:S(2)}, u32[]{:S(2)}) async-start(f32[4,2,36,516]{3,1,2,0:T(2,128)} %pad_maximum_fusion.1), calls=%async_computation | async-start | bytes 1474560 | tf_op jit(solution)/shard_map/all_to_all | solution.py:115
  52.1 3.9 %collective-permute-start.6 = (f32[2,134,3]{2,1,0:T(8,128)S(1)}, f32[2,134,3]{2,1,0:T(8,128)S(1)}, u32[]{:S(2)}, u32[]{:S(2)}) collective-permute-start(f32[2,134,3]{2,1,0:T(8,128)S(1)} %get-tuple-element.29), channel_id=1, source_target_pairs={{0,1},{1,2},{2,3},{4,5},{5,6},{6,7},{8,9},{9,10},{10,11},{12,13},{... | collective-permute-start | bytes 9656 | tf_op jit(solution)/shard_map/ppermute | solution.py:21
  56.0 1.5 %collective-permute-start.7 = (f32[2,134,3]{2,1,0:T(8,128)S(1)}, f32[2,134,3]{2,1,0:T(8,128)S(1)}, u32[]{:S(2)}, u32[]{:S(2)}) collective-permute-start(f32[2,134,3]{2,1,0:T(8,128)S(1)} %get-tuple-element.30), channel_id=1, source_target_pairs={{1,0},{2,1},{3,2},{5,4},{6,5},{7,6},{9,8},{10,9},{11,10},{13,12},{... | collective-permute-start | bytes 9656 | tf_op jit(solution)/shard_map/ppermute | solution.py:21
  57.5 9.2 %collective-permute-done.6 = f32[2,134,3]{2,1,0:T(8,128)S(1)} collective-permute-done((f32[2,134,3]{2,1,0:T(8,128)S(1)}, f32[2,134,3]{2,1,0:T(8,128)S(1)}, u32[]{:S(2)}, u32[]{:S(2)}) %collective-permute-start.6) | collective-permute-done | bytes 3248 | tf_op jit(solution)/shard_map/ppermute | solution.py:21
  66.7 0.3 pad_maximum_fusion.2
  67.1 4.3 %all-to-all-done = f32[4,2,36,516]{3,1,2,0:T(2,128)S(1)} async-done(((f32[4,2,36,516]{3,1,2,0:T(2,128)}), f32[4,2,36,516]{3,1,2,0:T(2,128)S(1)}, u32[]{:S(2)}, u32[]{:S(2)}) %all-to-all-start) | async-done | bytes 594464 | tf_op jit(solution)/shard_map/all_to_all | solution.py:115
  71.3 0.8 fusion.90
  72.2 0.3 copy.35
  72.7 0.7 fusion.32
  73.5 0.9 fusion.23
  74.4 1.4 %subtract_bitcast_fusion = (f32[1,1,128,512]{3,2,1,0:T(8,128)S(1)}, f32[128,512]{1,0:T(8,128)}) fusion(f32[128,512]{1,0:T(8,128)S(1)} %copy-done.2, f32[130,514]{1,0:T(8,128)S(1)} %fusion.23, f32[134,518]{1,0:T(8,128)S(1)} %get-tuple-element.23, f32[132,516]{1,0:T(8,128)S(1)} %get-tuple-element.10), kind=kLoop, calls=%fused_computation.124 | loop fusion | flops 1441792 | bytes 3407872
  75.9 0.3 copy.34
  76.1 0.5 pad_maximum_fusion.3
  76.6 15.6 %copy.24 = f32[2,65536]{0,1:T(8,128)} copy(f32[2,65536]{1,0:T(2,128)S(1)} %pad_maximum_fusion.3) | data formatting | bytes 1048576 | tf_op jit(solution)/shard_map/stack | solution.py:185
  92.2 18.2 %gather_fusion = f32[2048,2]{1,0:T(8,128)} fusion(f32[2,65536]{0,1:T(8,128)} %copy.24, s32[2048]{0:T(1024)S(1)} %fusion.79), kind=kCustom, calls=%fused_computation | custom fusion | bytes 40960 | tf_op jit(solution)/shard_map/gather | solution.py:186
  110.4 6.8 %scatter_custom_fusion = f32[3,6144]{0,1:T(8,128)S(1)} fusion(s32[2048]{0:T(1024)S(1)} %bitcast.102, f32[]{:T(128)} %constant.34.clone.1, f32[2,2048]{0,1:T(8,128)} %bitcast.96, f32[]{:T(128)} %constant.45.clone.1), kind=kCustom, calls=%fused_computation.28 | custom fusion | bytes 90120 | tf_op jit(solution)/shard_map/scatter | solution.py:188
  117.2 1.5 %copy.25 = f32[3,32,192]{2,0,1:T(4,128)S(1)} copy(f32[3,32,192]{0,2,1:T(8,128)S(1)} %bitcast.89) | data formatting | bytes 147456 | tf_op jit(solution)/shard_map/all_to_all | solution.py:189
  118.7 15.4 %all_to_all.14 = f32[3,32,192]{2,0,1:T(4,128)S(1)} all-to-all(f32[3,32,192]{2,0,1:T(4,128)S(1)} %copy.25), channel_id=1, replica_groups=mesh['gx'=8,'gy'=4] {'gx','gy'}, dimensions={1} | all-to-all | bytes 147456 | tf_op jit(solution)/shard_map/all_to_all | solution.py:189
  134.1 0.2 slice_reduce_fusion.2
  134.9 1.1 add_select_fusion
  136.1 0.7 pad_maximum_fusion.12
  (59 shorter events, 2.1 us)
Async XLA Ops:
  0.6 22.7 %copy-start = (f32[8,32,2048]{2,1,0:T(8,128)S(1)}, f32[8,32,2048]{2,1,0:T(8,128)}, u32[]{:S(2)}) copy-start(f32[8,32,2048]{2,1,0:T(8,128)} %param.11) | copy-start | bytes 6291460
  0.6 19.0 %copy-start.5 = (s32[2048,1]{0,1:T(1,128)S(1)}, s32[2048,1]{0,1:T(1,128)}, u32[]{:S(2)}) copy-start(s32[2048,1]{0,1:T(1,128)} %param.19) | copy-start | bytes 24580
  0.7 19.2 %copy-start.7 = (s32[2048]{0:T(1024)S(1)}, s32[2048]{0:T(1024)}, u32[]{:S(2)}) copy-start(s32[2048]{0:T(1024)} %param.18) | copy-start | bytes 24580
  3.5 16.3 %collective-permute-start = (f32[8,3,2048]{2,1,0:T(4,128)S(1)}, f32[8,3,2048]{2,1,0:T(4,128)S(1)}, u32[]{:S(2)}, u32[]{:S(2)}) collective-permute-start(f32[8,3,2048]{2,1,0:T(4,128)S(1)} %pad_maximum_fusion.5), channel_id=1, source_target_pairs={{0,1},{1,2},{2,3},{3,4},{4,5},{5,6},{6,7},{7,8},{8,9},{9,10},{10,1... | collective-permute-start | bytes 589832 | tf_op jit(solution)/shard_map/ppermute | solution.py:21
  8.6 14.6 %collective-permute-start.1 = (f32[8,3,2048]{2,1,0:T(4,128)S(1)}, f32[8,3,2048]{2,1,0:T(4,128)S(1)}, u32[]{:S(2)}, u32[]{:S(2)}) collective-permute-start(f32[8,3,2048]{2,1,0:T(4,128)S(1)} %pad_maximum_fusion.6), channel_id=1, source_target_pairs={{1,0},{2,1},{3,2},{4,3},{5,4},{6,5},{7,6},{8,7},{9,8},{10,9},{11,1... | collective-permute-start | bytes 589832 | tf_op jit(solution)/shard_map/ppermute | solution.py:21
  10.7 41.2 %collective-permute-start.4 = (f32[2,3,512]{2,1,0:T(4,128)S(1)}, f32[2,3,512]{2,1,0:T(4,128)S(1)}, u32[]{:S(2)}, u32[]{:S(2)}) collective-permute-start(f32[2,3,512]{2,1,0:T(4,128)S(1)} %get-tuple-element.31), channel_id=1, source_target_pairs={{0,4},{4,8},{8,12},{12,16},{16,20},{20,24},{24,28},{1,5},{5,9},{9,... | collective-permute-start | bytes 36872 | tf_op jit(solution)/shard_map/ppermute | solution.py:21
  15.4 36.5 %collective-permute-start.5 = (f32[2,3,512]{2,1,0:T(4,128)S(1)}, f32[2,3,512]{2,1,0:T(4,128)S(1)}, u32[]{:S(2)}, u32[]{:S(2)}) collective-permute-start(f32[2,3,512]{2,1,0:T(4,128)S(1)} %get-tuple-element.32), channel_id=1, source_target_pairs={{4,0},{8,4},{12,8},{16,12},{20,16},{24,20},{28,24},{5,1},{9,5},{13... | collective-permute-start | bytes 36872 | tf_op jit(solution)/shard_map/ppermute | solution.py:21
  19.9 3.8 %copy-start.8 = (f32[7]{0:T(128)S(1)}, f32[7]{0:T(128)}, u32[]{:S(2)}) copy-start(f32[7]{0:T(128)} %param.14) | copy-start | bytes 88
  23.7 1.6 %copy-start.1 = (f32[8,32,2048]{2,1,0:T(8,128)S(1)}, f32[8,32,2048]{2,1,0:T(8,128)}, u32[]{:S(2)}) copy-start(f32[8,32,2048]{2,1,0:T(8,128)} %param.12) | copy-start | bytes 6291460
  23.8 1.6 %copy-start.9 = (f32[8]{0:T(128)S(1)}, f32[8]{0:T(128)}, u32[]{:S(2)}) copy-start(f32[8]{0:T(128)} %param.13) | copy-start | bytes 100
  35.9 4.2 %collective-permute-start.2 = (f32[2,2048]{1,0:T(2,128)S(1)}, f32[2,2048]{1,0:T(2,128)S(1)}, u32[]{:S(2)}, u32[]{:S(2)}) collective-permute-start(f32[2,2048]{1,0:T(2,128)S(1)} %get-tuple-element.33), channel_id=1, source_target_pairs={{0,1},{1,2},{2,3},{3,4},{4,5},{5,6},{6,7},{7,8},{8,9},{9,10},{10,1... | collective-permute-start | bytes 49160 | tf_op jit(solution)/shard_map/ppermute | solution.py:21
  38.4 5.6 %collective-permute-start.3 = (f32[2,2048]{1,0:T(2,128)S(1)}, f32[2,2048]{1,0:T(2,128)S(1)}, u32[]{:S(2)}, u32[]{:S(2)}) collective-permute-start(f32[2,2048]{1,0:T(2,128)S(1)} %get-tuple-element.34), channel_id=1, source_target_pairs={{1,0},{2,1},{3,2},{4,3},{5,4},{6,5},{7,6},{8,7},{9,8},{10,9},{11,1... | collective-permute-start | bytes 49160 | tf_op jit(solution)/shard_map/ppermute | solution.py:21
  44.2 7.7 %copy-start.2 = (f32[128,512]{1,0:T(8,128)S(1)}, f32[128,512]{1,0:T(8,128)}, u32[]{:S(2)}) copy-start(f32[128,512]{1,0:T(8,128)} %param.17) | copy-start | bytes 786436
  44.2 7.7 %copy-start.3 = (f32[128,512]{1,0:T(8,128)S(1)}, f32[128,512]{1,0:T(8,128)}, u32[]{:S(2)}) copy-start(f32[128,512]{1,0:T(8,128)} %param.16) | copy-start | bytes 786436
  46.5 24.8 %all-to-all-start = ((f32[4,2,36,516]{3,1,2,0:T(2,128)}), f32[4,2,36,516]{3,1,2,0:T(2,128)S(1)}, u32[]{:S(2)}, u32[]{:S(2)}) async-start(f32[4,2,36,516]{3,1,2,0:T(2,128)} %pad_maximum_fusion.1), calls=%async_computation | async-start | bytes 1474560 | tf_op jit(solution)/shard_map/all_to_all | solution.py:115
  52.1 14.6 %collective-permute-start.6 = (f32[2,134,3]{2,1,0:T(8,128)S(1)}, f32[2,134,3]{2,1,0:T(8,128)S(1)}, u32[]{:S(2)}, u32[]{:S(2)}) collective-permute-start(f32[2,134,3]{2,1,0:T(8,128)S(1)} %get-tuple-element.29), channel_id=1, source_target_pairs={{0,1},{1,2},{2,3},{4,5},{5,6},{6,7},{8,9},{9,10},{10,11},{12,13},{... | collective-permute-start | bytes 9656 | tf_op jit(solution)/shard_map/ppermute | solution.py:21
  56.0 10.7 %collective-permute-start.7 = (f32[2,134,3]{2,1,0:T(8,128)S(1)}, f32[2,134,3]{2,1,0:T(8,128)S(1)}, u32[]{:S(2)}, u32[]{:S(2)}) collective-permute-start(f32[2,134,3]{2,1,0:T(8,128)S(1)} %get-tuple-element.30), channel_id=1, source_target_pairs={{1,0},{2,1},{3,2},{5,4},{6,5},{7,6},{9,8},{10,9},{11,10},{13,12},{... | collective-permute-start | bytes 9656 | tf_op jit(solution)/shard_map/ppermute | solution.py:21
  117.2 17.7 %copy-start.4 = (f32[2,1,6144]{2,1,0:T(1,128)S(1)}, f32[2,1,6144]{2,1,0:T(1,128)}, u32[]{:S(2)}) copy-start(f32[2,1,6144]{2,1,0:T(1,128)} %param.20) | copy-start | bytes 147460
  117.2 17.7 %copy-start.6 = (f32[1,6144]{1,0:T(1,128)S(1)}, f32[1,6144]{1,0:T(1,128)}, u32[]{:S(2)}) copy-start(f32[1,6144]{1,0:T(1,128)} %param.21) | copy-start | bytes 73732
where the time goes:
time: 137 us
  local copies, waits for them, and re-layouts  51 us (37%)
  starting transfers between devices  26.7 us (19%)
  waiting for transfers between devices  20.8 us (15%)
  other arithmetic  20.7 us (15%)
  blocking collectives  15.4 us (11%)
    ppermute x8, starting transfers between devices, exchange(): return (lax.ppermute(last, axis, up), lax.ppermute(leading, axis, down))  21.4 us
    gather x1, local copies, waits for them, and re-layouts, body(): picked = fields[:, joint_cell]  18.2 us
    ppermute x8, waiting for transfers between devices, exchange(): return (lax.ppermute(last, axis, up), lax.ppermute(leading, axis, down))  16.5 us
    another operation x1, local copies, waits for them, and re-layouts, body(): fields = jnp.stack([(warp - warp_prev).reshape(-1), top.reshape(-1)])  15.6 us
    all_to_all x1, blocking collectives, body(): lax.all_to_all(outgoing, FLAT, split_axis=1, concat_axis=1, tiled=True)  15.4 us
    scatter x1, local copies, waits for them, and re-layouts, body(): jnp.zeros((3, devices * capacity), jnp.float32).at[:, slots].set(values)  6.81 us
    all_to_all x1, starting transfers between devices, relay(): recv = lax.all_to_all(send, 'gy', split_axis=0, concat_axis=0, tiled=True)  5.38 us
    add x1, other arithmetic, moment_of(): total = total + weighting[layer] * field[layer]  5.21 us
  transfers between devices with their start and end apart: 9, of which 4 were waited for; matrix products, arithmetic and copies ran while one was open for 14% of the time, Pallas kernels for 0%

commit v1 on v0

--- a/solution.py
+++ b/solution.py
@@ -12,6 +12,28 @@
 sat_power = 0.3
 harden = 2.0
 FLAT = ("gx", "gy")
+
+
+def in_blocks(x, dim, size):
+    before, after = (x.shape[:dim], x.shape[dim + 1 :])
+    return jnp.moveaxis(x.reshape(*before, size, -1, *after), dim, 0)
+
+
+def in_order(pieces, dim):
+    pieces = jnp.moveaxis(pieces, 0, dim)
+    shape = pieces.shape
+    return pieces.reshape(*shape[:dim], shape[dim] * shape[dim + 1], *shape[dim + 2 :])
+
+
+def exchange_in_pairs(x, axis, split_dim, concat_dim):
+    devices, index = (lax.axis_size(axis), lax.axis_index(axis))
+    blocks = in_blocks(x, split_dim, devices)
+    outs = [blocks[index]]
+    for turn in range(1, devices):
+        sent = blocks[index ^ turn]
+        outs.append(lax.ppermute(sent, axis, [(i, i ^ turn) for i in range(devices)]))
+    blocks = jnp.stack(outs)[index ^ jnp.arange(devices)]
+    return in_order(blocks, concat_dim)
 
 
 def exchange(last, leading, axis):
@@ -112,7 +134,7 @@
     tp = jnp.pad(top, ((width, width), (width, width)))
     both = jnp.stack([lp, tp])
     send = jnp.stack([both[:, :, k * cm : k * cm + cm + 2 * width] for k in range(n_gy)])
-    recv = lax.all_to_all(send, "gy", split_axis=0, concat_axis=0, tiled=True)
+    recv = exchange_in_pairs(send, "gy", 0, 0)
     parts = []
     for k in range(n_gy):
         lo = 0 if k == 0 else width

time: 137 us -> 144 us (1.051)
  blocking collectives: 15.4 us -> 22.8 us
  waiting for transfers between devices: 20.8 us -> 15.8 us
  other arithmetic: 20.7 us -> 24.6 us
  starting transfers between devices: 26.7 us -> 29.2 us
    ppermute x8, waiting for transfers between devices: 16.5 us -> 5.66 us  [exchange(): return (lax.ppermute(last, axis, up), lax.ppermute(leading, axis, down))]
    ppermute x0 -> x3, waiting for transfers between devices: none -> 10.2 us  [exchange_in_pairs(): lax.ppermute(sent, axis, [(i, i ^ turn) for i in range(devices)])]
    all_to_all x1, blocking collectives: 15.4 us -> 22.8 us  [body(): lax.all_to_all(outgoing, FLAT, split_axis=1, concat_axis=1, tiled=True)]
    all_to_all x1 -> x0, starting transfers between devices: 5.38 us -> none  [relay(): recv = lax.all_to_all(send, 'gy', split_axis=0, concat_axis=0, tiled=True)]
    ppermute x0 -> x3, starting transfers between devices: none -> 4.65 us  [exchange_in_pairs(): lax.ppermute(sent, axis, [(i, i ^ turn) for i in range(devices)])]
    all_to_all x1 -> x0, waiting for transfers between devices: 4.28 us -> none  [relay(): recv = lax.all_to_all(send, 'gy', split_axis=0, concat_axis=0, tiled=True)]
    ppermute x8, starting transfers between devices: 21.4 us -> 24.5 us  [exchange(): return (lax.ppermute(last, axis, up), lax.ppermute(leading, axis, down))]
    another operation x2, other arithmetic: 1.89 us -> 0.13 us  [relay(): jnp.stack([both[:, :, k * cm:k * cm + cm + 2 * width] for k in range(n_gy)])]
  transfers between devices with their start and end apart: 9 -> 11, of which waited for: 4 -> 6; matrix products, arithmetic and copies ran while one was open for 14% -> 6% of each run, Pallas kernels for 0% -> 0%
where the time goes in v1:
time: 144 us
  local copies, waits for them, and re-layouts  49.9 us (35%)
  starting transfers between devices  29.2 us (20%)
  other arithmetic  24.6 us (17%)
  blocking collectives  22.8 us (16%)
  waiting for transfers between devices  15.8 us (11%)
    ppermute x8, starting transfers between devices, exchange(): return (lax.ppermute(last, axis, up), lax.ppermute(leading, axis, down))  24.5 us
    all_to_all x1, blocking collectives, body(): lax.all_to_all(outgoing, FLAT, split_axis=1, concat_axis=1, tiled=True)  22.8 us
    gather x1, local copies, waits for them, and re-layouts, body(): picked = fields[:, joint_cell]  18.1 us
    another operation x1, local copies, waits for them, and re-layouts, body(): fields = jnp.stack([(warp - warp_prev).reshape(-1), top.reshape(-1)])  15.6 us
    ppermute x3, waiting for transfers between devices, exchange_in_pairs(): lax.ppermute(sent, axis, [(i, i ^ turn) for i in range(devices)])  10.2 us
    scatter x1, local copies, waits for them, and re-layouts, body(): jnp.zeros((3, devices * capacity), jnp.float32).at[:, slots].set(values)  6.8 us
    ppermute x8, waiting for transfers between devices, exchange(): return (lax.ppermute(last, axis, up), lax.ppermute(leading, axis, down))  5.66 us
    add x1, other arithmetic, moment_of(): total = total + weighting[layer] * field[layer]  5.15 us
  transfers between devices with their start and end apart: 11, of which 6 were waited for; matrix products, arithmetic and copies ran while one was open for 6% of the time, Pallas kernels for 0%

profile of v1, /device:TPU:0, one launch (start us, length us, event | category | flops | bytes accessed | tf_op | source)
XLA Modules:
  0.0 143.8 jit_solution(8150656457417252597)
XLA Ops:
  0.7 1.4 fusion.89
  2.1 1.3 fusion.90
  3.5 5.0 %collective-permute-start = (f32[8,3,2048]{2,0,1:T(8,128)S(1)}, f32[8,3,2048]{2,0,1:T(8,128)S(1)}, u32[]{:S(2)}, u32[]{:S(2)}) collective-permute-start(f32[8,3,2048]{2,0,1:T(8,128)S(1)} %pad_maximum_fusion.6), channel_id=1, source_target_pairs={{0,1},{1,2},{2,3},{3,4},{4,5},{5,6},{6,7},{7,8},{8,9},{9,10},{10,1... | collective-permute-start | bytes 589832 | tf_op jit(solution)/shard_map/ppermute | solution.py:43
  8.6 1.3 collective-permute-start.1
  9.9 0.9 pad_maximum_fusion.14
  10.9 4.7 %collective-permute-start.7 = (f32[2,3,512]{2,1,0:T(4,128)S(1)}, f32[2,3,512]{2,1,0:T(4,128)S(1)}, u32[]{:S(2)}, u32[]{:S(2)}) collective-permute-start(f32[2,3,512]{2,1,0:T(4,128)S(1)} %get-tuple-element.35), channel_id=1, source_target_pairs={{0,4},{4,8},{8,12},{12,16},{16,20},{20,24},{24,28},{1,5},{5,9},{9,... | collective-permute-start | bytes 36872 | tf_op jit(solution)/shard_map/ppermute | solution.py:43
  15.5 1.3 collective-permute-start.8
  16.8 0.6 fusion.86
  17.4 0.6 fusion.85
  18.0 0.7 fusion.92
  18.7 0.6 pad_clamp_fusion
  19.3 0.5 compare_and_fusion
  20.6 0.6 compare_select_fusion.1
  21.2 0.6 compare_and_fusion.1
  21.8 0.8 pad_maximum_fusion.11
  22.6 1.3 collective-permute-start.10
  23.9 5.2 %collective-permute-start.9 = (f32[2,134,3]{2,1,0:T(8,128)}, f32[2,134,3]{2,1,0:T(8,128)}, u32[]{:S(2)}, u32[]{:S(2)}) collective-permute-start(f32[2,134,3]{2,1,0:T(8,128)} %get-tuple-element.33), channel_id=1, source_target_pairs={{0,1},{1,2},{2,3},{4,5},{5,6},{6,7},{8,9},{9,10},{10,11},{12,13},{... | collective-permute-start | bytes 9656 | tf_op jit(solution)/shard_map/ppermute | solution.py:43
  29.1 0.6 compare_and_fusion.2
  29.8 1.6 %collective-permute-done.9 = f32[2,134,3]{2,1,0:T(8,128)} collective-permute-done((f32[2,134,3]{2,1,0:T(8,128)}, f32[2,134,3]{2,1,0:T(8,128)}, u32[]{:S(2)}, u32[]{:S(2)}) %collective-permute-start.9) | collective-permute-done | bytes 3248 | tf_op jit(solution)/shard_map/ppermute | solution.py:43
  31.4 1.2 pad_maximum_fusion.2
  33.1 0.4 pad_maximum_fusion
  33.6 0.5 fusion.8
  34.1 1.1 copy-done.1
  35.2 3.0 %fusion.7 = f32[8,34,2048]{2,1,0:T(8,128)S(1)} fusion(f32[8,36,2048]{2,1,0:T(8,128)S(1)} %pad_maximum_fusion, f32[8,2,2048]{2,1,0:T(2,128)S(1)} %copy.22, f32[8,32,2048]{2,1,0:T(8,128)S(1)} %copy-done, f32[8,2,2048]{2,1,0:T(2,128)S(1)} %copy.21, f32[8,1,2048]{2,1,0:T(1,128)S(1)} %copy.26, f32[8,32,2048]{2,1,0:T(8,128)S(1)} %copy-done.1, ...), kind=kLoop, calls=%fused_computation.14 | loop fusion | flops 8355840 | bytes 14353408 | tf_op jit(solution)/shard_map/jit(_where)/select_n | solution.py:123
  38.3 0.4 fusion.16
  38.6 2.0 %fusion.15 = f32[8,32,2048]{2,1,0:T(8,128)S(1)} fusion(f32[8,32,2048]{2,1,0:T(8,128)S(1)} %copy-done.1, f32[8,34,2048]{2,1,0:T(8,128)S(1)} %fusion.7, f32[7,32,2048]{2,1,0:T(8,128)S(1)} %fusion.16, f32[8]{0:T(128)S(1)} %copy-done.12), kind=kLoop, calls=%fused_computation.25 | loop fusion | flops 5242880 | bytes 14942720 | tf_op jit(solution)/shard_map/add | solution.py:62
  40.7 5.2 %fusion.54 = f32[32,2048]{1,0:T(8,128)S(1)} fusion(f32[8,32,2048]{2,1,0:T(8,128)S(1)} %fusion.15, f32[]{:T(128)} %bitcast.8, f32[]{:T(128)} %bitcast.6, f32[]{:T(128)} %bitcast.5, f32[]{:T(128)} %bitcast.4, f32[]{:T(128)} %bitcast.3, f32[]{:T(128)} %bitcast.2, f32[]{:T(128)} %bitcast.1, f32[]{:T(128)} %bitcast), kind=kLoop, calls=%fused_computation.112 | loop fusion | flops 983040 | bytes 2359328 | tf_op jit(solution)/shard_map/add | solution.py:68
  45.9 4.4 %collective-permute-start.2 = (f32[2,2048]{1,0:T(2,128)S(1)}, f32[2,2048]{1,0:T(2,128)S(1)}, u32[]{:S(2)}, u32[]{:S(2)}) collective-permute-start(f32[2,2048]{1,0:T(2,128)S(1)} %get-tuple-element.37), channel_id=1, source_target_pairs={{0,1},{1,2},{2,3},{3,4},{4,5},{5,6},{6,7},{7,8},{8,9},{9,10},{10,1... | collective-permute-start | bytes 49160 | tf_op jit(solution)/shard_map/ppermute | solution.py:43
  50.2 1.5 %collective-permute-start.3 = (f32[2,2048]{1,0:T(2,128)S(1)}, f32[2,2048]{1,0:T(2,128)S(1)}, u32[]{:S(2)}, u32[]{:S(2)}) collective-permute-start(f32[2,2048]{1,0:T(2,128)S(1)} %get-tuple-element.38), channel_id=1, source_target_pairs={{1,0},{2,1},{3,2},{4,3},{5,4},{6,5},{7,6},{8,7},{9,8},{10,9},{11,1... | collective-permute-start | bytes 49160 | tf_op jit(solution)/shard_map/ppermute | solution.py:43
  51.9 4.0 %collective-permute-done.3 = f32[2,2048]{1,0:T(2,128)S(1)} collective-permute-done((f32[2,2048]{1,0:T(2,128)S(1)}, f32[2,2048]{1,0:T(2,128)S(1)}, u32[]{:S(2)}, u32[]{:S(2)}) %collective-permute-start.3) | collective-permute-done | bytes 16416 | tf_op jit(solution)/shard_map/ppermute | solution.py:43
  56.4 4.6 %collective-permute-start.5 = (f32[1,2,36,516]{3,2,1,0:T(8,128)S(1)}, f32[1,2,36,516]{3,2,1,0:T(8,128)S(1)}, u32[]{:S(2)}, u32[]{:S(2)}) collective-permute-start(f32[1,2,36,516]{3,2,1,0:T(8,128)S(1)} %get-tuple-element.25), channel_id=1, source_target_pairs={{0,2},{1,3},{2,0},{3,1},{4,6},{5,7},{6,4},{7,5},{8,10},{9,11},{10,... | collective-permute-start | bytes 445832 | tf_op jit(solution)/shard_map/ppermute | solution.py:34
  61.0 4.2 %collective-permute-done.4 = f32[1,2,36,516]{3,2,1,0:T(8,128)S(1)} collective-permute-done((f32[1,2,36,516]{3,2,1,0:T(8,128)S(1)}, f32[1,2,36,516]{3,2,1,0:T(8,128)S(1)}, u32[]{:S(2)}, u32[]{:S(2)}) %collective-permute-start.4) | collective-permute-done | bytes 148640 | tf_op jit(solution)/shard_map/ppermute | solution.py:34
  65.1 2.7 %collective-permute-done.5 = f32[1,2,36,516]{3,2,1,0:T(8,128)S(1)} collective-permute-done((f32[1,2,36,516]{3,2,1,0:T(8,128)S(1)}, f32[1,2,36,516]{3,2,1,0:T(8,128)S(1)}, u32[]{:S(2)}, u32[]{:S(2)}) %collective-permute-start.5) | collective-permute-done | bytes 148640 | tf_op jit(solution)/shard_map/ppermute | solution.py:34
  67.9 3.3 %collective-permute-done.6 = f32[1,2,36,516]{3,2,1,0:T(8,128)S(1)} collective-permute-done((f32[1,2,36,516]{3,2,1,0:T(8,128)S(1)}, f32[1,2,36,516]{3,2,1,0:T(8,128)S(1)}, u32[]{:S(2)}, u32[]{:S(2)}) %collective-permute-start.6) | collective-permute-done | bytes 148640 | tf_op jit(solution)/shard_map/ppermute | solution.py:34
  71.2 0.7 gather_fusion
  72.2 0.3 copy.34
  72.5 0.7 fusion.32
  73.2 0.9 fusion.23
  74.2 1.4 subtract_bitcast_fusion
  75.6 0.3 copy.33
  75.9 0.5 pad_maximum_fusion.3
  76.4 15.6 %copy.27 = f32[2,65536]{0,1:T(8,128)} copy(f32[2,65536]{1,0:T(2,128)S(1)} %pad_maximum_fusion.3) | data formatting | bytes 1048576 | tf_op jit(solution)/shard_map/stack | solution.py:207
  91.9 18.1 %gather_fusion.1 = f32[2048,2]{1,0:T(8,128)} fusion(f32[2,65536]{0,1:T(8,128)} %copy.27, s32[2048]{0:T(1024)S(1)} %fusion.79), kind=kCustom, calls=%fused_computation.1 | custom fusion | bytes 40960 | tf_op jit(solution)/shard_map/gather | solution.py:208
  110.0 6.8 %scatter_custom_fusion = f32[3,6144]{0,1:T(8,128)S(1)} fusion(s32[2048]{0:T(1024)} %bitcast.116, f32[]{:T(128)} %constant.37.clone.1, f32[2,2048]{0,1:T(8,128)} %bitcast.107, f32[]{:T(128)} %constant.51.clone.1), kind=kCustom, calls=%fused_computation.29 | custom fusion | bytes 1123328 | tf_op jit(solution)/shard_map/scatter | solution.py:210
  116.9 1.5 %copy.28 = f32[3,32,192]{2,0,1:T(4,128)S(1)} copy(f32[3,32,192]{0,2,1:T(8,128)S(1)} %bitcast.100) | data formatting | bytes 147456 | tf_op jit(solution)/shard_map/all_to_all | solution.py:211
  118.4 22.8 %all_to_all.9 = f32[3,32,192]{2,0,1:T(4,128)S(1)} all-to-all(f32[3,32,192]{2,0,1:T(4,128)S(1)} %copy.28), channel_id=1, replica_groups=mesh['gx'=8,'gy'=4] {'gx','gy'}, dimensions={1} | all-to-all | bytes 147456 | tf_op jit(solution)/shard_map/all_to_all | solution.py:211
  141.9 1.1 add_select_fusion
  143.1 0.7 pad_maximum_fusion.12
  (86 shorter events, 3.5 us)
Async XLA Ops:
  0.6 21.2 %copy-start.2 = (f32[128,512]{1,0:T(8,128)S(1)}, f32[128,512]{1,0:T(8,128)}, u32[]{:S(2)}) copy-start(f32[128,512]{1,0:T(8,128)} %param.17) | copy-start | bytes 786436
  0.6 21.2 %copy-start.3 = (f32[128,512]{1,0:T(8,128)S(1)}, f32[128,512]{1,0:T(8,128)}, u32[]{:S(2)}) copy-start(f32[128,512]{1,0:T(8,128)} %param.16) | copy-start | bytes 786436
  0.7 17.4 %copy-start.8 = (f32[8]{0:T(128)S(1)}, f32[8]{0:T(128)}, u32[]{:S(2)}) copy-start(f32[8]{0:T(128)} %param.15) | copy-start | bytes 100
  0.7 19.1 %copy-start.10 = (s32[2048]{0:T(1024)S(1)}, s32[2048]{0:T(1024)}, u32[]{:S(2)}) copy-start(s32[2048]{0:T(1024)} %param.18) | copy-start | bytes 24580
  0.7 19.1 %copy-start.5 = (s32[2048,1]{0,1:T(1,128)S(1)}, s32[2048,1]{0,1:T(1,128)}, u32[]{:S(2)}) copy-start(s32[2048,1]{0,1:T(1,128)} %param.19) | copy-start | bytes 24580
  3.5 29.1 %collective-permute-start = (f32[8,3,2048]{2,0,1:T(8,128)S(1)}, f32[8,3,2048]{2,0,1:T(8,128)S(1)}, u32[]{:S(2)}, u32[]{:S(2)}) collective-permute-start(f32[8,3,2048]{2,0,1:T(8,128)S(1)} %pad_maximum_fusion.6), channel_id=1, source_target_pairs={{0,1},{1,2},{2,3},{3,4},{4,5},{5,6},{6,7},{7,8},{8,9},{9,10},{10,1... | collective-permute-start | bytes 589832 | tf_op jit(solution)/shard_map/ppermute | solution.py:43
  8.6 24.1 %collective-permute-start.1 = (f32[8,3,2048]{2,0,1:T(8,128)S(1)}, f32[8,3,2048]{2,0,1:T(8,128)S(1)}, u32[]{:S(2)}, u32[]{:S(2)}) collective-permute-start(f32[8,3,2048]{2,0,1:T(8,128)S(1)} %pad_maximum_fusion.7), channel_id=1, source_target_pairs={{1,0},{2,1},{3,2},{4,3},{5,4},{6,5},{7,6},{8,7},{9,8},{10,9},{11,1... | collective-permute-start | bytes 589832 | tf_op jit(solution)/shard_map/ppermute | solution.py:43
  9.9 23.2 %copy-start = (f32[8,32,2048]{2,1,0:T(8,128)S(1)}, f32[8,32,2048]{2,1,0:T(8,128)}, u32[]{:S(2)}) copy-start(f32[8,32,2048]{2,1,0:T(8,128)} %param.11) | copy-start | bytes 6291460
  10.9 10.9 %collective-permute-start.7 = (f32[2,3,512]{2,1,0:T(4,128)S(1)}, f32[2,3,512]{2,1,0:T(4,128)S(1)}, u32[]{:S(2)}, u32[]{:S(2)}) collective-permute-start(f32[2,3,512]{2,1,0:T(4,128)S(1)} %get-tuple-element.35), channel_id=1, source_target_pairs={{0,4},{4,8},{8,12},{12,16},{16,20},{20,24},{24,28},{1,5},{5,9},{9,... | collective-permute-start | bytes 36872 | tf_op jit(solution)/shard_map/ppermute | solution.py:43
  15.5 6.3 %collective-permute-start.8 = (f32[2,3,512]{2,1,0:T(4,128)S(1)}, f32[2,3,512]{2,1,0:T(4,128)S(1)}, u32[]{:S(2)}, u32[]{:S(2)}) collective-permute-start(f32[2,3,512]{2,1,0:T(4,128)S(1)} %get-tuple-element.36), channel_id=1, source_target_pairs={{4,0},{8,4},{12,8},{16,12},{20,16},{24,20},{28,24},{5,1},{9,5},{13... | collective-permute-start | bytes 36872 | tf_op jit(solution)/shard_map/ppermute | solution.py:43
  21.8 0.8 copy-start.6
  21.8 0.8 copy-start.7
  22.6 7.1 %collective-permute-start.10 = (f32[2,134,3]{2,1,0:T(8,128)}, f32[2,134,3]{2,1,0:T(8,128)S(1)}, u32[]{:S(2)}, u32[]{:S(2)}) collective-permute-start(f32[2,134,3]{2,1,0:T(8,128)} %get-tuple-element.34), channel_id=1, source_target_pairs={{1,0},{2,1},{3,2},{5,4},{6,5},{7,6},{9,8},{10,9},{11,10},{13,12},{... | collective-permute-start | bytes 9656 | tf_op jit(solution)/shard_map/ppermute | solution.py:43
  23.9 7.5 %collective-permute-start.9 = (f32[2,134,3]{2,1,0:T(8,128)}, f32[2,134,3]{2,1,0:T(8,128)}, u32[]{:S(2)}, u32[]{:S(2)}) collective-permute-start(f32[2,134,3]{2,1,0:T(8,128)} %get-tuple-element.33), channel_id=1, source_target_pairs={{0,1},{1,2},{2,3},{4,5},{5,6},{6,7},{8,9},{9,10},{10,11},{12,13},{... | collective-permute-start | bytes 9656 | tf_op jit(solution)/shard_map/ppermute | solution.py:43
  33.0 0.7 copy-start.11
  33.6 1.6 %copy-start.1 = (f32[8,32,2048]{2,1,0:T(8,128)S(1)}, f32[8,32,2048]{2,1,0:T(8,128)}, u32[]{:S(2)}) copy-start(f32[8,32,2048]{2,1,0:T(8,128)} %param.12) | copy-start | bytes 6291460
  33.6 1.6 %copy-start.12 = (f32[8]{0:T(128)S(1)}, f32[8]{0:T(128)}, u32[]{:S(2)}) copy-start(f32[8]{0:T(128)} %param.13) | copy-start | bytes 100
  33.6 1.6 %copy-start.16 = (pred[34]{0:T(512)(128)(4,1)S(1)}, pred[34]{0:T(512)(128)(4,1)}, u32[]{:S(2)}) copy-start(pred[34]{0:T(512)(128)(4,1)} %compare_and_fusion.2) | copy-start | bytes 106
  45.9 6.0 %collective-permute-start.2 = (f32[2,2048]{1,0:T(2,128)S(1)}, f32[2,2048]{1,0:T(2,128)S(1)}, u32[]{:S(2)}, u32[]{:S(2)}) collective-permute-start(f32[2,2048]{1,0:T(2,128)S(1)} %get-tuple-element.37), channel_id=1, source_target_pairs={{0,1},{1,2},{2,3},{3,4},{4,5},{5,6},{6,7},{7,8},{8,9},{9,10},{10,1... | collective-permute-start | bytes 49160 | tf_op jit(solution)/shard_map/ppermute | solution.py:43
  50.2 5.6 %collective-permute-start.3 = (f32[2,2048]{1,0:T(2,128)S(1)}, f32[2,2048]{1,0:T(2,128)S(1)}, u32[]{:S(2)}, u32[]{:S(2)}) collective-permute-start(f32[2,2048]{1,0:T(2,128)S(1)} %get-tuple-element.38), channel_id=1, source_target_pairs={{1,0},{2,1},{3,2},{4,3},{5,4},{6,5},{7,6},{8,7},{9,8},{10,9},{11,1... | collective-permute-start | bytes 49160 | tf_op jit(solution)/shard_map/ppermute | solution.py:43
  56.3 8.9 %collective-permute-start.4 = (f32[1,2,36,516]{3,2,1,0:T(8,128)S(1)}, f32[1,2,36,516]{3,2,1,0:T(8,128)S(1)}, u32[]{:S(2)}, u32[]{:S(2)}) collective-permute-start(f32[1,2,36,516]{3,2,1,0:T(8,128)S(1)} %get-tuple-element.26), channel_id=1, source_target_pairs={{0,1},{1,0},{2,3},{3,2},{4,5},{5,4},{6,7},{7,6},{8,9},{9,8},{10,11... | collective-permute-start | bytes 445832 | tf_op jit(solution)/shard_map/ppermute | solution.py:34
  56.4 11.5 %collective-permute-start.5 = (f32[1,2,36,516]{3,2,1,0:T(8,128)S(1)}, f32[1,2,36,516]{3,2,1,0:T(8,128)S(1)}, u32[]{:S(2)}, u32[]{:S(2)}) collective-permute-start(f32[1,2,36,516]{3,2,1,0:T(8,128)S(1)} %get-tuple-element.25), channel_id=1, source_target_pairs={{0,2},{1,3},{2,0},{3,1},{4,6},{5,7},{6,4},{7,5},{8,10},{9,11},{10,... | collective-permute-start | bytes 445832 | tf_op jit(solution)/shard_map/ppermute | solution.py:34
  60.9 10.2 %collective-permute-start.6 = (f32[1,2,36,516]{3,2,1,0:T(8,128)S(1)}, f32[1,2,36,516]{3,2,1,0:T(8,128)S(1)}, u32[]{:S(2)}, u32[]{:S(2)}) collective-permute-start(f32[1,2,36,516]{3,2,1,0:T(8,128)S(1)} %get-tuple-element.24), channel_id=1, source_target_pairs={{0,3},{1,2},{2,1},{3,0},{4,7},{5,6},{6,5},{7,4},{8,11},{9,10},{10,... | collective-permute-start | bytes 445832 | tf_op jit(solution)/shard_map/ppermute | solution.py:34
  71.1 1.3 copy-start.14
  71.1 1.3 copy-start.15
  72.1 1.1 copy-start.13
  72.1 1.1 copy-start.17
  116.9 25.1 %copy-start.4 = (f32[2,1,6144]{2,1,0:T(1,128)S(1)}, f32[2,1,6144]{2,1,0:T(1,128)}, u32[]{:S(2)}) copy-start(f32[2,1,6144]{2,1,0:T(1,128)} %param.20) | copy-start | bytes 147460
  116.9 25.1 %copy-start.9 = (f32[1,6144]{1,0:T(1,128)S(1)}, f32[1,6144]{1,0:T(1,128)}, u32[]{:S(2)}) copy-start(f32[1,6144]{1,0:T(1,128)} %param.21) | copy-start | bytes 73732
